TPU v7x, 256 devices: a whole 4x4x8 slice. The times are simulated.
256 devices in a mesh: dp: 16 (over z, core), tensor: 16 (over y, x).
Axes of the slice: x: 4, y: 4, z: 8, core: 2. Of those that a mesh axis runs over, the one named last changes fastest.
Arguments:
- tokens: bfloat16 [8192, 2048], P(('dp', 'tensor')), may hold values from -6 to 6
- lengths: int32 [16, 8], P('dp'), may hold values from 1 to 128, 512 in all within a row
- group_prefix: int32 [16], replicated, may hold values from 0 to 15, as said below
- prefix_cache: bfloat16 [65536, 512], P(('dp', 'tensor')), may hold values from -340 to 340
- query_weight: bfloat16 [2048, 1024], P(None, 'tensor'), may hold values from -0.125 to 0.125
- key_weight: bfloat16 [2048, 256], replicated, may hold values from -0.375 to 0.375
- value_weight: bfloat16 [2048, 256], replicated, may hold values from -0.125 to 0.125
- out_weight: bfloat16 [1024, 2048], P('tensor'), may hold values from -0.1875 to 0.1875
- gate_up_weight: bfloat16 [2, 2048, 5120], P(None, None, 'tensor'), may hold values from -0.125 to 0.125
- down_weight: bfloat16 [5120, 2048], P('tensor'), may hold values from -0.078125 to 0.078125
Outputs:
- layer_out: bfloat16 [8192, 2048], P(('dp', 'tensor'))
Inputs may be any that keep to these rules, and one draw needn't show every extreme that they name: The 8 lengths of a group sum to 512, and one of them is exactly 128. `group_prefix`: several groups may continue the same slot.
All inputs are finite; a program needn't handle non-finite values.
Results may differ from a plain program's by a relative error of at most 0.023.
Values may be sent and summed in bfloat16 or wider, within the bound.
No kernel may reach another device: no remote copies, remote signals or barrier semaphores. Data moves between devices by JAX's collectives and lax.ppermute only.
A program may use at most 64 MiB of HBM per device.

v0:
```python
import math
import jax
import jax.numpy as jnp
from jax import lax
from jax.sharding import PartitionSpec as P

QH = 16
KVH = 4
HD = 64
PLEN = 4096
NEG_FILL = -1e30


def token_layout(lengths, total_rows):
    ends_at = jnp.cumsum(lengths)
    starts_at = ends_at - lengths
    indices = jnp.arange(total_rows, dtype=jnp.int32)
    request = jnp.sum((indices[:, None] >= ends_at[None, :]).astype(jnp.int32), axis=1)
    begins = jnp.max(
        jnp.where(starts_at[None, :] <= indices[:, None], starts_at[None, :], 0), axis=1
    )
    return ((PLEN + indices - begins).astype(jnp.float32), request)


def rope_tables(positions):
    halves = HD // 2
    steps_float = jnp.arange(halves, dtype=jnp.float32)
    inverse = jnp.exp(steps_float * (-2.0 * math.log(10000.0) / HD))
    angles = positions[:, None] * inverse[None, :]
    return (jnp.cos(angles), jnp.sin(angles))


def rotate(values, cos_table, sin_table):
    halves = values.shape[-1] // 2
    former = values[..., :halves]
    latter = values[..., halves:]
    cos_rows = cos_table[:, None, :]
    sin_rows = sin_table[:, None, :]
    return jnp.concatenate(
        [former * cos_rows - latter * sin_rows, latter * cos_rows + former * sin_rows], axis=-1
    )


def norm_rows(inputs):
    floats = inputs.astype(jnp.float32)
    return (floats * lax.rsqrt(jnp.mean(floats * floats, axis=-1, keepdims=True) + 1e-05)).astype(
        jnp.bfloat16
    )


def softmax_block(queries, keys_block, values_block, scaling, allowed):
    scores = (
        jnp.einsum("thd,nhd->thn", queries, keys_block, preferred_element_type=jnp.float32)
        * scaling
    )
    if allowed is not None:
        scores = jnp.where(allowed, scores, NEG_FILL)
    top_score = jnp.max(scores, axis=2)
    exponent = jnp.exp(scores - top_score[:, :, None])
    weight = jnp.sum(exponent, axis=2)
    blended = jnp.einsum(
        "thn,nhd->thd",
        exponent.astype(jnp.bfloat16),
        values_block,
        preferred_element_type=jnp.float32,
    )
    return (top_score, weight, blended)


def merge_states(former, latter):
    top_one, weight_one, blend_one = former
    top_two, weight_two, blend_two = latter
    overall = jnp.maximum(top_one, top_two)
    factor_one = jnp.exp(top_one - overall)
    factor_two = jnp.exp(top_two - overall)
    return (
        overall,
        weight_one * factor_one + weight_two * factor_two,
        blend_one * factor_one[:, :, None] + blend_two * factor_two[:, :, None],
    )


def on_device(
    tokens,
    lengths,
    group_prefix,
    prefix_cache,
    query_weight,
    key_weight,
    value_weight,
    out_weight,
    gate_up_weight,
    down_weight,
):
    tensor_count = lax.axis_size("tensor")
    tensor_rank = lax.axis_index("tensor")
    group_rank = lax.axis_index("dp")
    row_count = tokens.shape[0]
    group_tokens = row_count * tensor_count
    local_heads = query_weight.shape[1] // HD
    head_ratio = QH // KVH
    local_kv = max(1, local_heads // head_ratio)
    repeat_by = local_heads // local_kv
    kv_first = tensor_rank * local_heads // head_ratio
    kv_total = KVH * HD
    query_width = local_heads * HD
    kv_width = local_kv * HD
    scaling = 1.0 / math.sqrt(HD)
    positions, request = token_layout(lengths[0], group_tokens)
    cos_table, sin_table = rope_tables(positions)
    key_cols = lax.dynamic_slice_in_dim(key_weight, kv_first * HD, kv_width, 1)
    value_cols = lax.dynamic_slice_in_dim(value_weight, kv_first * HD, kv_width, 1)
    projection = jnp.concatenate([query_weight, key_cols, value_cols], axis=1)
    normed = norm_rows(tokens)
    segment = lax.all_gather(normed, "tensor", axis=0, tiled=True)
    seg_rows = segment.shape[0]
    mapped = jnp.dot(segment, projection, preferred_element_type=jnp.float32)
    query_part = rotate(
        mapped[:, :query_width].reshape(seg_rows, local_heads, HD), cos_table, sin_table
    )
    key_part = rotate(
        mapped[:, query_width : query_width + kv_width].reshape(seg_rows, local_kv, HD),
        cos_table,
        sin_table,
    )
    projected = jnp.concatenate(
        [
            query_part.reshape(seg_rows, query_width),
            key_part.reshape(seg_rows, kv_width),
            mapped[:, query_width + kv_width :],
        ],
        axis=1,
    ).astype(jnp.bfloat16)
    queries = projected[:, :query_width].reshape(group_tokens, local_heads, HD)
    own_keys = jnp.repeat(
        projected[:, query_width : query_width + kv_width].reshape(group_tokens, local_kv, HD),
        repeat_by,
        axis=1,
    )
    own_values = jnp.repeat(
        projected[:, query_width + kv_width :].reshape(group_tokens, local_kv, HD),
        repeat_by,
        axis=1,
    )
    slot_wanted = group_prefix[group_rank]
    shard_rows = prefix_cache.shape[0]
    segment = lax.all_gather(prefix_cache, "dp", axis=0, tiled=True)
    seg_rows = segment.shape[0]
    indices = jnp.arange(seg_rows, dtype=jnp.int32)
    matches = indices // shard_rows == slot_wanted
    places = indices % shard_rows
    chosen = (
        jnp.zeros_like(prefix_cache)
        .at[places]
        .add(jnp.where(matches[:, None], segment, jnp.zeros_like(segment)))
    )
    start_state = (
        jnp.full((group_tokens, local_heads), NEG_FILL, jnp.float32),
        jnp.zeros((group_tokens, local_heads), jnp.float32),
        jnp.zeros((group_tokens, local_heads, HD), jnp.float32),
    )
    segment = lax.all_gather(chosen, "tensor", axis=0, tiled=True)
    seg_rows = segment.shape[0]
    keys_block = lax.dynamic_slice_in_dim(segment, kv_first * HD, kv_width, 1).reshape(
        seg_rows, local_kv, HD
    )
    values_block = lax.dynamic_slice_in_dim(segment, kv_total + kv_first * HD, kv_width, 1).reshape(
        seg_rows, local_kv, HD
    )
    keys_block = jnp.repeat(keys_block, repeat_by, axis=1)
    values_block = jnp.repeat(values_block, repeat_by, axis=1)
    prefix_state = merge_states(
        start_state, softmax_block(queries, keys_block, values_block, scaling, None)
    )
    indices = jnp.arange(group_tokens, dtype=jnp.int32)
    allowed = (request[:, None] == request[None, :]) & (indices[None, :] <= indices[:, None])
    suffix_state = softmax_block(queries, own_keys, own_values, scaling, allowed[:, None, :])
    top_score, weight, blended = merge_states(prefix_state, suffix_state)
    attended = (
        (blended / weight[:, :, None]).astype(jnp.bfloat16).reshape(group_tokens, query_width)
    )
    attn_sum = lax.psum_scatter(
        jnp.dot(attended, out_weight, preferred_element_type=jnp.float32).astype(jnp.bfloat16),
        "tensor",
        scatter_dimension=0,
        tiled=True,
    ).astype(jnp.float32)
    middle = (tokens.astype(jnp.float32) + attn_sum).astype(jnp.bfloat16)
    segment = lax.all_gather(norm_rows(middle), "tensor", axis=0, tiled=True)
    gate_value = jnp.dot(segment, gate_up_weight[0], preferred_element_type=jnp.float32)
    upward = jnp.dot(segment, gate_up_weight[1], preferred_element_type=jnp.float32)
    hidden = (jax.nn.silu(gate_value) * upward).astype(jnp.bfloat16)
    ffn_sum = lax.psum_scatter(
        jnp.dot(hidden, down_weight, preferred_element_type=jnp.float32).astype(jnp.bfloat16),
        "tensor",
        scatter_dimension=0,
        tiled=True,
    ).astype(jnp.float32)
    return (middle.astype(jnp.float32) + ffn_sum).astype(jnp.bfloat16)


def solution(mesh):
    return jax.shard_map(
        on_device,
        mesh=mesh,
        in_specs=(
            P(("dp", "tensor"), None),
            P("dp", None),
            P(),
            P(("dp", "tensor"), None),
            P(None, "tensor"),
            P(),
            P(),
            P("tensor", None),
            P(None, None, "tensor"),
            P("tensor", None),
        ),
        out_specs=P(("dp", "tensor"), None),
        check_vma=False,
    )
```

profile of v0, /device:TPU:32, one launch (start us, length us, event | category | flops | bytes accessed | tf_op | source)
XLA Modules:
  0.0 400.2 jit_solution(4943395580398315689)
XLA Ops:
  6.5 0.0 copy-start
  6.5 0.0 all-gather.5.cloned.1.call-start
  6.5 0.7 all-gather.5.cloned.1.call-update
  7.3 0.0 all-gather.9.cloned.1.call-start
  7.3 1.0 fusion.66
  8.3 0.0 copy-start.5
  8.4 0.0 copy-start.3
  8.4 1.7 fusion.67
  10.1 0.0 all-gather.9.cloned.1.call-update
  10.1 0.0 all-gather.7.cloned.1.call-start
  10.1 1.2 dynamic_slice.15
  11.4 0.6 fusion.93
  12.0 41.6 %all-gather.5.cloned.1.call-done = bf16[4096,512]{1,0:T(8,128)(2,1)} async-done(((bf16[256,512]{1,0:T(8,128)(2,1)}), bf16[4096,512]{1,0:T(8,128)(2,1)}) %all-gather.5.cloned.1.call-update) | async-done | bytes 4194320 | tf_op jit(solution)/shard_map/all_gather | solution.py:147
  53.6 28.1 %scatter_custom_fusion = bf16[256,512]{1,0:T(8,128)(2,1)} fusion(s32[4096]{0:T(1024)S(1)} %bitcast.114, bf16[4096,512]{1,0:T(8,128)(2,1)} %all-gather.5.cloned.1.call-done, pred[4096]{0:T(1024)(128)(4,1)S(1)} %fusion.93, bf16[]{:T(256)} %constant.71.clone.1), kind=kCustom, calls=%fused_computation.7 | custom fusion | flops 4194304 | bytes 4461568 | tf_op jit(solution)/shard_map/scatter-add | solution.py:155
  81.8 0.0 all-gather.7.cloned.1.call-update
  81.8 0.0 reduce-scatter.3.cloned.1.call-start
  81.9 0.0 copy-done.5
  81.9 0.2 reduce-window.4
  82.1 0.0 copy-done.3
  82.1 0.3 copy.13
  82.4 0.1 select_reduce_fusion
  82.5 0.1 convert_reduce_fusion
  82.5 1.6 constant_dynamic-slice_fusion
  84.1 20.8 %all-gather.9.cloned.1.call-done = bf16[512,2048]{1,0:T(8,128)(2,1)} async-done(((bf16[32,2048]{1,0:T(8,128)(2,1)}), bf16[512,2048]{1,0:T(8,128)(2,1)}) %all-gather.9.cloned.1.call-update) | async-done | bytes 2097168 | tf_op jit(solution)/shard_map/all_gather | solution.py:115
  104.9 2.7 fusion.41
  107.7 0.3 fusion.86
  108.0 0.4 fusion.112
  108.4 0.2 fusion.51
  108.6 54.8 %all-gather.7.cloned.1.call-done = bf16[4096,512]{1,0:T(8,128)(2,1)} async-done(((bf16[256,512]{1,0:T(8,128)(2,1)}), bf16[4096,512]{1,0:T(8,128)(2,1)}) %all-gather.7.cloned.1.call-update) | async-done | bytes 4194320 | tf_op jit(solution)/shard_map/all_gather | solution.py:162
  163.4 2.5 multiply_reduce_fusion
  165.9 1.4 fusion.1
  167.4 0.0 copy-start.4
  167.4 3.1 fusion.36
  170.5 0.0 copy-done.4
  170.5 0.0 copy-start.1
  170.5 2.3 convolution_convert_fusion.1
  172.8 0.0 reduce-scatter.3.cloned.1.call-update
  172.9 0.0 all-gather.11.cloned.1.call-start
  172.9 79.3 %reduce-scatter.3.cloned.1.call-done = bf16[32,2048]{1,0:T(8,128)(2,1)} async-done(((bf16[512,2048]{1,0:T(8,128)(2,1)}), bf16[32,2048]{1,0:T(8,128)(2,1)}) %reduce-scatter.3.cloned.1.call-update) | async-done | bytes 131088 | tf_op jit(solution)/shard_map/reduce_scatter | solution.py:182
  252.2 0.0 copy-done.1
  252.2 1.1 fusion.69
  253.3 1.7 fusion.70
  255.0 0.0 all-gather.11.cloned.1.call-update
  255.0 0.2 reduce-scatter.5.cloned.1.call-start
  255.2 49.2 %all-gather.11.cloned.1.call-done = bf16[512,2048]{1,0:T(8,128)(2,1)} async-done(((bf16[32,2048]{1,0:T(8,128)(2,1)}), bf16[512,2048]{1,0:T(8,128)(2,1)}) %all-gather.11.cloned.1.call-update) | async-done | bytes 2097168 | tf_op jit(solution)/shard_map/all_gather | solution.py:189
  304.4 2.8 fusion.13
  307.2 0.0 copy-done
  307.2 0.0 copy-start.2
  307.2 5.5 %convolution_convert_fusion = bf16[512,2048]{1,0:T(8,128)(2,1)} fusion(bf16[320,2048]{1,0:T(8,128)(2,1)S(1)} %copy-done, bf16[512,2048]{1,0:T(8,128)(2,1)} %all-gather.11.cloned.1.call-done, bf16[2,2048,320]{1,2,0:T(8,128)(2,1)} %param.18, f32[512,320]{0,1:T(8,128)S(1)} %fusion.13), kind=kOutput, calls=%fused_computation.11 | convolution fusion | flops 1344208896 | bytes 7471104 | tf_op jit(solution)/shard_map/dot_general | solution.py:194
  312.7 0.0 reduce-scatter.5.cloned.1.call-update
  312.7 79.0 %reduce-scatter.5.cloned.1.call-done = bf16[32,2048]{1,0:T(8,128)(2,1)} async-done(((bf16[512,2048]{1,0:T(8,128)(2,1)}), bf16[32,2048]{1,0:T(8,128)(2,1)}) %reduce-scatter.5.cloned.1.call-update) | async-done | bytes 131088 | tf_op jit(solution)/shard_map/reduce_scatter | solution.py:193
  391.7 0.0 copy-done.2
  391.7 1.6 fusion.71
  (8 shorter events, 0.1 us)
Async XLA Ops:
  6.5 300.7 %copy-start = (bf16[320,2048]{1,0:T(8,128)(2,1)S(1)}, bf16[320,2048]{1,0:T(8,128)(2,1)}, u32[]{:S(2)}) copy-start(bf16[320,2048]{1,0:T(8,128)(2,1)} %param.19) | copy-start | bytes 3932164
  6.5 47.1 %all-gather.5.cloned.1.call-start = ((), (), s32[]{:S(2)}) async-start(), calls=%async_computation.2 | async-start | bytes 4456448 | tf_op jit(solution)/shard_map/all_gather | solution.py:147
  7.3 97.7 %all-gather.9.cloned.1.call-start = ((), (), s32[]{:S(2)}) async-start(), calls=%async_computation.4 | async-start | bytes 2228224 | tf_op jit(solution)/shard_map/all_gather | solution.py:115
  8.3 73.5 %copy-start.5 = (s32[1,8]{1,0:T(1,128)S(1)}, s32[1,8]{1,0:T(1,128)}, u32[]{:S(2)}) copy-start(s32[1,8]{1,0:T(1,128)} %param.11) | copy-start | bytes 100
  8.4 73.7 %copy-start.3 = (bf16[2048,64]{0,1:T(8,128)(2,1)S(1)}, bf16[2048,64]{0,1:T(8,128)(2,1)}, u32[]{:S(2)}) copy-start(bf16[2048,64]{0,1:T(8,128)(2,1)} %param.14) | copy-start | bytes 786436
  10.1 153.3 %all-gather.7.cloned.1.call-start = ((), (), s32[]{:S(2)}) async-start(), calls=%async_computation.3 | async-start | bytes 4456448 | tf_op jit(solution)/shard_map/all_gather | solution.py:162
  81.8 170.5 %reduce-scatter.3.cloned.1.call-start = ((), (), s32[]{:S(2)}) async-start(), calls=%async_computation.5 | async-start | bytes 2228224 | tf_op jit(solution)/shard_map/reduce_scatter | solution.py:182
  167.4 3.1 copy-start.4
  170.5 81.7 %copy-start.1 = (bf16[32,2048]{1,0:T(8,128)(2,1)S(1)}, bf16[32,2048]{1,0:T(8,128)(2,1)}, u32[]{:S(2)}) copy-start(bf16[32,2048]{1,0:T(8,128)(2,1)} %param.10) | copy-start | bytes 393220
  172.9 131.5 %all-gather.11.cloned.1.call-start = ((), (), s32[]{:S(2)}) async-start(), calls=%async_computation.6 | async-start | bytes 2228224 | tf_op jit(solution)/shard_map/all_gather | solution.py:189
  255.0 136.8 %reduce-scatter.5.cloned.1.call-start = ((), (), s32[]{:S(2)}) async-start(), calls=%async_computation.7 | async-start | bytes 2228224 | tf_op jit(solution)/shard_map/reduce_scatter | solution.py:193
  307.2 84.5 %copy-start.2 = (bf16[32,2048]{1,0:T(8,128)(2,1)S(1)}, bf16[32,2048]{1,0:T(8,128)(2,1)}, u32[]{:S(2)}) copy-start(bf16[32,2048]{1,0:T(8,128)(2,1)} %reduce-scatter.3.cloned.1.call-done) | copy-start | bytes 393220
Sparse Core Ops, SparseCore 0:
  9.2 44.4 all-gather.4
  56.1 48.8 all-gather.8
  107.4 55.9 all-gather.6
  173.0 79.2 reduce-scatter.2
  255.1 49.2 all-gather.10
  312.9 78.8 reduce-scatter.4
where the time goes:
time: 401 us; the launch traced here: 400 us
  waiting for transfers between devices  325 us (81%)
  other arithmetic  38.2 us (10%)
  matrix products  19.4 us (5%)
  between operations  13.7 us (3%)
    reduce_scatter x1, waiting for transfers between devices, on_device(): lax.psum_scatter(jnp.dot(attended, out_weight, preferred_element_type=jnp...  79.3 us
    reduce_scatter x1, waiting for transfers between devices, on_device(): lax.psum_scatter(jnp.dot(hidden, down_weight, preferred_element_type=jnp....  79 us
    all_gather x1, waiting for transfers between devices, on_device(): segment = lax.all_gather(chosen, 'tensor', axis=0, tiled=True)  54.8 us
    all_gather x1, waiting for transfers between devices, on_device(): segment = lax.all_gather(norm_rows(middle), 'tensor', axis=0, tiled=True)  49.2 us
    all_gather x1, waiting for transfers between devices, on_device(): segment = lax.all_gather(prefix_cache, 'dp', axis=0, tiled=True)  41.6 us
    scatter-add x1, other arithmetic, on_device(): chosen = jnp.zeros_like(prefix_cache).at[places].add(jnp.where(matches[:,...  28.1 us
    all_gather x1, waiting for transfers between devices, on_device(): segment = lax.all_gather(normed, 'tensor', axis=0, tiled=True)  20.8 us
  transfers between devices with their start and end apart: 6, of which 6 were waited for; matrix products, arithmetic and copies ran while one was open for 10% of the time, Pallas kernels for 0%

commit v1 on v0

--- a/solution.py
+++ b/solution.py
@@ -112,7 +112,8 @@
     value_cols = lax.dynamic_slice_in_dim(value_weight, kv_first * HD, kv_width, 1)
     projection = jnp.concatenate([query_weight, key_cols, value_cols], axis=1)
     normed = norm_rows(tokens)
-    segment = lax.all_gather(normed, "tensor", axis=0, tiled=True)
+    copies = jnp.concatenate([normed] * lax.axis_size("tensor"), axis=0)
+    segment = lax.all_to_all(copies, "tensor", 0, 0, tiled=True)
     seg_rows = segment.shape[0]
     mapped = jnp.dot(segment, projection, preferred_element_type=jnp.float32)
     query_part = rotate(

time: 401 us -> 393 us (0.980)
  waiting for transfers between devices: 325 us -> 292 us
  other arithmetic: 38.2 us -> 52.9 us
  starting transfers between devices: 0.39 us -> 7.29 us
    all_gather x1, waiting for transfers between devices: 54.8 us -> 16.8 us  [on_device(): segment = lax.all_gather(chosen, 'tensor', axis=0, tiled=True)]
    all_to_all x0 -> x1, waiting for transfers between devices: none -> 31.8 us  [on_device(): segment = lax.all_to_all(copies, 'tensor', 0, 0, tiled=True)]
    all_gather x1 -> x0, waiting for transfers between devices: 20.8 us -> none  [on_device(): segment = lax.all_gather(normed, 'tensor', axis=0, tiled=True)]
    unnamed x0 -> x15, other arithmetic: none -> 15.6 us
    all_to_all x0 -> x1, starting transfers between devices: none -> 6.94 us  [on_device(): segment = lax.all_to_all(copies, 'tensor', 0, 0, tiled=True)]
    all_gather x1, waiting for transfers between devices: 41.6 us -> 35.2 us  [on_device(): segment = lax.all_gather(prefix_cache, 'dp', axis=0, tiled=True)]
  transfers between devices with their start and end apart: 6 -> 6, of which waited for: 6 -> 6; matrix products, arithmetic and copies ran while one was open for 10% -> 7% of each run, Pallas kernels for 0% -> 0%
where the time goes in v1:
time: 393 us; the launch traced here: 392 us
  waiting for transfers between devices  292 us (74%)
  other arithmetic  52.9 us (13%)
  matrix products  20.8 us (5%)
  between operations  13.3 us (3%)
  starting transfers between devices  7.29 us (2%)
  local copies, waits for them, and re-layouts  6.19 us (2%)
    reduce_scatter x1, waiting for transfers between devices, on_device(): lax.psum_scatter(jnp.dot(attended, out_weight, preferred_element_type=jnp...  79.2 us
    reduce_scatter x1, waiting for transfers between devices, on_device(): lax.psum_scatter(jnp.dot(hidden, down_weight, preferred_element_type=jnp....  79 us
    all_gather x1, waiting for transfers between devices, on_device(): segment = lax.all_gather(norm_rows(middle), 'tensor', axis=0, tiled=True)  49.2 us
    all_gather x1, waiting for transfers between devices, on_device(): segment = lax.all_gather(prefix_cache, 'dp', axis=0, tiled=True)  35.2 us
    all_to_all x1, waiting for transfers between devices, on_device(): segment = lax.all_to_all(copies, 'tensor', 0, 0, tiled=True)  31.8 us
    scatter-add x1, other arithmetic, on_device(): chosen = jnp.zeros_like(prefix_cache).at[places].add(jnp.where(matches[:,...  28.2 us
    all_gather x1, waiting for transfers between devices, on_device(): segment = lax.all_gather(chosen, 'tensor', axis=0, tiled=True)  16.8 us
    unnamed x15, other arithmetic  15.6 us
  transfers between devices with their start and end apart: 6, of which 6 were waited for; matrix products, arithmetic and copies ran while one was open for 7% of the time, Pallas kernels for 0%

profile of v1, /device:TPU:32, one launch (start us, length us, event | category | flops | bytes accessed | tf_op | source)
XLA Modules:
  0.0 392.4 jit_solution(11126090918031395237)
XLA Ops:
  6.5 0.0 copy-start
  6.5 0.0 all-gather.4.cloned.1.call-start
  6.5 0.7 all-gather.4.cloned.1.call-update
  7.3 0.0 all-gather.6.cloned.1.call-start
  7.3 1.2 dynamic_slice.15
  8.6 0.7 fusion.93
  9.2 1.0 fusion.66
  10.3 1.6 constant_dynamic-update-slice_fusion.15
  11.9 1.6 constant_dynamic-update-slice_fusion.14
  13.6 1.6 constant_dynamic-update-slice_fusion.13
  15.2 1.6 constant_dynamic-update-slice_fusion.12
  16.8 1.6 constant_dynamic-update-slice_fusion.11
  18.5 35.2 %all-gather.4.cloned.1.call-done = bf16[4096,512]{1,0:T(8,128)(2,1)} async-done(((bf16[256,512]{1,0:T(8,128)(2,1)}), bf16[4096,512]{1,0:T(8,128)(2,1)}) %all-gather.4.cloned.1.call-update) | async-done | bytes 4194320 | tf_op jit(solution)/shard_map/all_gather | solution.py:148
  53.6 28.2 %scatter_custom_fusion = bf16[256,512]{1,0:T(8,128)(2,1)} fusion(s32[4096]{0:T(1024)S(1)} %bitcast.117, bf16[4096,512]{1,0:T(8,128)(2,1)} %all-gather.4.cloned.1.call-done, pred[4096]{0:T(1024)(128)(4,1)S(1)} %fusion.93, bf16[]{:T(256)} %constant.71.clone.1), kind=kCustom, calls=%fused_computation.7 | custom fusion | flops 4194304 | bytes 4461568 | tf_op jit(solution)/shard_map/scatter-add | solution.py:156
  81.8 0.0 all-gather.6.cloned.1.call-update
  81.8 0.0 copy-done.1
  81.8 0.7 constant_dynamic-update-slice_fusion.10
  82.6 0.7 constant_dynamic-update-slice_fusion.9
  83.3 0.7 constant_dynamic-update-slice_fusion.8
  84.0 0.7 constant_dynamic-update-slice_fusion.7
  84.8 0.7 constant_dynamic-update-slice_fusion.6
  85.5 0.8 constant_dynamic-update-slice_fusion.5
  86.3 0.7 constant_dynamic-update-slice_fusion.4
  87.0 0.7 constant_dynamic-update-slice_fusion.3
  87.7 0.7 constant_dynamic-update-slice_fusion.2
  88.5 0.7 constant_dynamic-update-slice_fusion.1
  89.2 0.7 constant_dynamic-update-slice_fusion
  90.0 6.9 %all-to-all-start = ((bf16[16,32,2048]{2,1,0:T(8,128)(2,1)}), bf16[16,32,2048]{2,1,0:T(8,128)(2,1)S(1)}, u32[]{:S(2)}, u32[]{:S(2)}) async-start(bf16[16,32,2048]{2,1,0:T(8,128)(2,1)} %bitcast.2), calls=%async_computation | async-start | bytes 4194304 | tf_op jit(solution)/shard_map/all_to_all | solution.py:116
  96.9 0.0 reduce-scatter.3.cloned.1.call-start
  97.0 0.0 copy-done.6
  97.0 0.2 reduce-window.4
  97.2 1.9 copy.13
  99.1 0.1 select_reduce_fusion
  99.2 0.1 convert_reduce_fusion
  99.3 2.6 constant_dynamic-slice_fusion
  101.9 31.8 %all-to-all-done = bf16[16,32,2048]{2,1,0:T(8,128)(2,1)S(1)} async-done(((bf16[16,32,2048]{2,1,0:T(8,128)(2,1)}), bf16[16,32,2048]{2,1,0:T(8,128)(2,1)S(1)}, u32[]{:S(2)}, u32[]{:S(2)}) %all-to-all-start) | async-done | bytes 2097184 | tf_op jit(solution)/shard_map/all_to_all | solution.py:116
  133.7 2.8 fusion.41
  136.5 0.0 copy-start.3
  136.5 0.3 fusion.86
  136.8 0.4 copy-done.3
  137.2 0.4 fusion.112
  137.6 0.2 fusion.51
  137.8 16.8 %all-gather.6.cloned.1.call-done = bf16[4096,512]{1,0:T(8,128)(2,1)} async-done(((bf16[256,512]{1,0:T(8,128)(2,1)}), bf16[4096,512]{1,0:T(8,128)(2,1)}) %all-gather.6.cloned.1.call-update) | async-done | bytes 4194320 | tf_op jit(solution)/shard_map/all_gather | solution.py:163
  154.6 2.5 multiply_reduce_fusion
  157.2 1.4 fusion.1
  158.6 0.0 copy-start.4
  158.7 3.1 fusion.36
  161.7 0.0 copy-done.4
  161.8 3.2 convolution_convert_fusion.1
  165.0 0.0 reduce-scatter.3.cloned.1.call-update
  165.0 0.0 all-gather.8.cloned.1.call-start
  165.1 79.2 %reduce-scatter.3.cloned.1.call-done = bf16[32,2048]{1,0:T(8,128)(2,1)} async-done(((bf16[512,2048]{1,0:T(8,128)(2,1)}), bf16[32,2048]{1,0:T(8,128)(2,1)}) %reduce-scatter.3.cloned.1.call-update) | async-done | bytes 131088 | tf_op jit(solution)/shard_map/reduce_scatter | solution.py:183
  244.3 1.1 fusion.69
  245.4 1.7 fusion.70
  247.0 0.0 all-gather.8.cloned.1.call-update
  247.0 0.2 reduce-scatter.5.cloned.1.call-start
  247.3 49.2 %all-gather.8.cloned.1.call-done = bf16[512,2048]{1,0:T(8,128)(2,1)} async-done(((bf16[32,2048]{1,0:T(8,128)(2,1)}), bf16[512,2048]{1,0:T(8,128)(2,1)}) %all-gather.8.cloned.1.call-update) | async-done | bytes 2097168 | tf_op jit(solution)/shard_map/all_gather | solution.py:190
  296.5 3.8 fusion.13
  300.3 0.0 copy-done
  300.3 0.0 copy-done.5
  300.3 5.0 %convolution_convert_fusion = bf16[512,2048]{1,0:T(8,128)(2,1)} fusion(bf16[320,2048]{1,0:T(8,128)(2,1)S(1)} %copy-done, bf16[512,2048]{1,0:T(8,128)(2,1)S(1)} %copy-done.5, bf16[2,2048,320]{1,2,0:T(8,128)(2,1)} %param.18, f32[512,320]{0,1:T(8,128)} %fusion.13), kind=kOutput, calls=%fused_computation.11 | convolution fusion | flops 1344208896 | bytes 7471104 | tf_op jit(solution)/shard_map/dot_general | solution.py:195
  305.2 0.0 reduce-scatter.5.cloned.1.call-update
  305.3 79.0 %reduce-scatter.5.cloned.1.call-done = bf16[32,2048]{1,0:T(8,128)(2,1)} async-done(((bf16[512,2048]{1,0:T(8,128)(2,1)}), bf16[32,2048]{1,0:T(8,128)(2,1)}) %reduce-scatter.5.cloned.1.call-update) | async-done | bytes 131088 | tf_op jit(solution)/shard_map/reduce_scatter | solution.py:194
  384.3 1.6 fusion.71
  (13 shorter events, 0.1 us)
Async XLA Ops:
  6.5 293.7 %copy-start = (bf16[320,2048]{1,0:T(8,128)(2,1)S(1)}, bf16[320,2048]{1,0:T(8,128)(2,1)}, u32[]{:S(2)}) copy-start(bf16[320,2048]{1,0:T(8,128)(2,1)} %param.19) | copy-start | bytes 3932164
  6.5 47.1 %all-gather.4.cloned.1.call-start = ((), (), s32[]{:S(2)}) async-start(), calls=%async_computation.3 | async-start | bytes 4456448 | tf_op jit(solution)/shard_map/all_gather | solution.py:148
  7.3 147.4 %all-gather.6.cloned.1.call-start = ((), (), s32[]{:S(2)}) async-start(), calls=%async_computation.4 | async-start | bytes 4456448 | tf_op jit(solution)/shard_map/all_gather | solution.py:163
  53.6 28.2 %copy-start.1 = (bf16[32,2048]{1,0:T(8,128)(2,1)S(1)}, bf16[32,2048]{1,0:T(8,128)(2,1)}, u32[]{:S(2)}) copy-start(bf16[32,2048]{1,0:T(8,128)(2,1)} %param.10) | copy-start | bytes 393220
  90.0 7.0 %copy-start.6 = (s32[1,8]{1,0:T(1,128)S(1)}, s32[1,8]{1,0:T(1,128)}, u32[]{:S(2)}) copy-start(s32[1,8]{1,0:T(1,128)} %param.11) | copy-start | bytes 100
  90.0 43.7 %all-to-all-start = ((bf16[16,32,2048]{2,1,0:T(8,128)(2,1)}), bf16[16,32,2048]{2,1,0:T(8,128)(2,1)S(1)}, u32[]{:S(2)}, u32[]{:S(2)}) async-start(bf16[16,32,2048]{2,1,0:T(8,128)(2,1)} %bitcast.2), calls=%async_computation | async-start | bytes 4194304 | tf_op jit(solution)/shard_map/all_to_all | solution.py:116
  96.9 147.4 %reduce-scatter.3.cloned.1.call-start = ((), (), s32[]{:S(2)}) async-start(), calls=%async_computation.5 | async-start | bytes 2228224 | tf_op jit(solution)/shard_map/reduce_scatter | solution.py:183
  136.5 0.8 copy-start.3
  158.6 3.1 copy-start.4
  165.0 131.4 %all-gather.8.cloned.1.call-start = ((), (), s32[]{:S(2)}) async-start(), calls=%async_computation.6 | async-start | bytes 2228224 | tf_op jit(solution)/shard_map/all_gather | solution.py:190
  247.0 137.2 %reduce-scatter.5.cloned.1.call-start = ((), (), s32[]{:S(2)}) async-start(), calls=%async_computation.7 | async-start | bytes 2228224 | tf_op jit(solution)/shard_map/reduce_scatter | solution.py:194
  296.5 3.8 copy-start.5
  305.2 79.0 %copy-start.2 = (bf16[32,2048]{1,0:T(8,128)(2,1)S(1)}, bf16[32,2048]{1,0:T(8,128)(2,1)}, u32[]{:S(2)}) copy-start(bf16[32,2048]{1,0:T(8,128)(2,1)} %reduce-scatter.3.cloned.1.call-done) | copy-start | bytes 393220
Sparse Core Ops, SparseCore 0:
  9.2 44.4 all-gather.3
  81.9 72.6 all-gather.5
  165.1 79.0 reduce-scatter.2
  247.2 49.2 all-gather.7
  305.4 78.8 reduce-scatter.4
